TPU v7x, 512 devices: a whole 4x4x16 slice. The times are simulated.
512 devices in a mesh: row: 32 (over z, core), col: 16 (over y, x).
Axes of the slice: x: 4, y: 4, z: 16, core: 2. Of those that a mesh axis runs over, the one named last changes fastest.
Arguments:
- inv_top: float32 [2, 4096, 4096], P(None, 'row', 'col'), may hold values from -0.0625 to 0.0625
- inv_bottom: float32 [2, 4096, 4096], P(None, 'row', 'col'), may hold values from -0.0625 to 0.0625
- lower_panel: float32 [2, 4096, 4096], P(None, 'row', 'col'), may hold values from -0.0625 to 0.0625
- rhs_top: float32 [2, 4096, 128], P(None, 'col'), may hold values from -6 to 6
- rhs_bottom: float32 [2, 4096, 128], P(None, 'row'), may hold values from -6 to 6
- source_xy: float32 [2, 2, 4096], P(None, None, 'col'), may hold values from -20 to 20
- source_depth: float32 [2, 4096], P(None, 'col'), may hold values from -2 to -0.5
- body_label: int32 [2, 4096], P(None, 'col'), may hold values 0 or 1
- field_xy: float32 [2, 98304], P(None, 'row'), may hold values from -20 to 20
- region_label: int32 [98304], P('row'), may hold values 0 or 1
- lid_table: float32 [2, 2], replicated, may hold values from 0.3 to 3
- wave_number: float32 [1], replicated, may hold values from 0.5 to 1.5
Outputs:
- strengths: float32 [2, 2, 4096, 128], P(None, None, 'col')
- elevation: float32 [98304, 2, 128], P(('row', 'col'))
All inputs are finite; a program needn't handle non-finite values. No bound on the sum of `body_label` or of `region_label` on one device may be relied on, other than what follows from the above.
Results may differ from a plain program's by a relative error of at most 0.004.
Values sent between devices are 32-bit elements; how exact they have to be, the bound alone decides.
No kernel may reach another device: no remote copies, remote signals or barrier semaphores. Data moves between devices by JAX's collectives and lax.ppermute only.
A program may use at most 64 MiB of HBM per device.

v0:
```python
import jax
import jax.numpy as jnp
from jax import lax
from jax.sharding import PartitionSpec as P


def complex_product(matrix, vector):
    highest = lax.Precision.HIGHEST
    real_part = jnp.dot(
        matrix[0], vector[0], precision=highest, preferred_element_type=jnp.float32
    ) - jnp.dot(matrix[1], vector[1], precision=highest, preferred_element_type=jnp.float32)
    imag_part = jnp.dot(
        matrix[0], vector[1], precision=highest, preferred_element_type=jnp.float32
    ) + jnp.dot(matrix[1], vector[0], precision=highest, preferred_element_type=jnp.float32)
    return jnp.stack([real_part, imag_part])


def green_tile(
    point_x, point_y, region, source_x, source_y, src_depth, src_label, lid_table, wave_value
):
    delta_x = point_x[:, None] - source_x[None, :]
    delta_y = point_y[:, None] - source_y[None, :]
    distance = jnp.sqrt(delta_x * delta_x + delta_y * delta_y + (src_depth * src_depth)[None, :])
    lid_first = jnp.where(region == 1, lid_table[1, 0], lid_table[0, 0])
    lid_second = jnp.where(region == 1, lid_table[1, 1], lid_table[0, 1])
    factor = jnp.where(src_label[None, :] == 1, lid_second[:, None], lid_first[:, None])
    amplitude = factor * jnp.exp(wave_value * src_depth)[None, :] / distance
    phase_angle = wave_value * distance
    return (
        (amplitude * jnp.cos(phase_angle)).astype(jnp.bfloat16),
        (amplitude * jnp.sin(phase_angle)).astype(jnp.bfloat16),
    )


def per_device(
    inv_top,
    inv_bottom,
    lower_panel,
    rhs_top,
    rhs_bottom,
    source_xy,
    source_depth,
    body_label,
    field_xy,
    region_label,
    lid_table,
    wave_number,
):
    col_rows = rhs_top.shape[1]

    def to_columns(row_block):
        gathered = lax.all_gather(row_block, "row", axis=1, tiled=True)
        return lax.dynamic_slice_in_dim(gathered, lax.axis_index("col") * col_rows, col_rows, 1)

    def column_total(partial_sum):
        return lax.psum(partial_sum, "col")

    top_solved = to_columns(column_total(complex_product(inv_top, rhs_top)))
    remainder = rhs_bottom - column_total(complex_product(lower_panel, top_solved))
    bottom_solved = to_columns(column_total(complex_product(inv_bottom, to_columns(remainder))))
    strengths = jnp.stack([top_solved, bottom_solved])
    weights = strengths.astype(jnp.bfloat16)
    right_count = weights.shape[3]
    src_real = weights[:, 0].reshape(-1, right_count)
    src_imag = weights[:, 1].reshape(-1, right_count)
    source_x = source_xy[0].reshape(-1)
    source_y = source_xy[1].reshape(-1)
    src_depth = source_depth.reshape(-1)
    src_label = body_label.reshape(-1)
    wave_value = wave_number[0]
    out_rows = field_xy.shape[1] // lax.axis_size("col")

    def block_term(first_row, block_rows):
        point_x = lax.dynamic_slice_in_dim(field_xy[0], first_row, block_rows)
        point_y = lax.dynamic_slice_in_dim(field_xy[1], first_row, block_rows)
        region = lax.dynamic_slice_in_dim(region_label, first_row, block_rows)
        tile_real, tile_imag = green_tile(
            point_x,
            point_y,
            region,
            source_x,
            source_y,
            src_depth,
            src_label,
            lid_table,
            wave_value,
        )
        real_part = jnp.dot(tile_real, src_real, preferred_element_type=jnp.float32) - jnp.dot(
            tile_imag, src_imag, preferred_element_type=jnp.float32
        )
        imag_part = jnp.dot(tile_real, src_imag, preferred_element_type=jnp.float32) + jnp.dot(
            tile_imag, src_real, preferred_element_type=jnp.float32
        )
        return jnp.stack([real_part, imag_part], axis=1)

    unit_count = out_rows * lax.axis_size("col") // out_rows
    group_units = max(
        (
            divisor
            for divisor in range(1, unit_count + 1)
            if unit_count % divisor == 0 and divisor * out_rows <= max(512, out_rows)
        )
    )
    block_rows = group_units * out_rows
    steps_count = out_rows * lax.axis_size("col") // block_rows

    def one_block(block_index):
        return block_term(block_index * block_rows, block_rows)

    results = lax.map(one_block, jnp.arange(steps_count, dtype=jnp.int32))
    elevation = lax.psum_scatter(
        results.reshape(out_rows * lax.axis_size("col"), 2, right_count),
        "col",
        scatter_dimension=0,
        tiled=True,
    )
    return (strengths, elevation)


def solution(mesh):
    in_specs = (
        P(None, "row", "col"),
        P(None, "row", "col"),
        P(None, "row", "col"),
        P(None, "col", None),
        P(None, "row", None),
        P(None, None, "col"),
        P(None, "col"),
        P(None, "col"),
        P(None, "row"),
        P("row"),
        P(),
        P(),
    )
    out_specs = (P(None, None, "col", None), P(("row", "col"), None, None))
    return jax.shard_map(
        per_device, mesh=mesh, in_specs=in_specs, out_specs=out_specs, check_vma=False
    )
```

profile of v0, /device:TPU:1, one launch (start us, length us, event | category | flops | bytes accessed | tf_op | source)
XLA Modules:
  0.0 916.5 jit_solution(3563913874649831330)
XLA Ops:
  13.0 117.3 %all-reduce.6.cloned.1.call-done = f32[2,128,128]{2,1,0:T(8,128)} async-done(((f32[2,128,128]{2,1,0:T(8,128)}), f32[2,128,128]{2,1,0:T(8,128)}) %all-reduce.6.cloned.1.call-update) | async-done | bytes 131088 | tf_op jit(solution)/shard_map/psum | solution.py:56
  130.4 77.4 %all-gather.4.cloned.1.call-done = f32[2,4096,128]{2,1,0:T(8,128)} async-done(((f32[2,128,128]{2,1,0:T(8,128)}), f32[2,4096,128]{2,1,0:T(8,128)}) %all-gather.4.cloned.1.call-update) | async-done | bytes 4194320 | tf_op jit(solution)/shard_map/all_gather | solution.py:52
  215.0 107.6 %all-reduce.8.cloned.1.call-done = f32[2,128,128]{1,2,0:T(8,128)} async-done(((f32[2,128,128]{1,2,0:T(8,128)}), f32[2,128,128]{1,2,0:T(8,128)}) %all-reduce.8.cloned.1.call-update) | async-done | bytes 131088 | tf_op jit(solution)/shard_map/psum | solution.py:56
  324.2 83.4 %all-gather.6.cloned.1.call-done = f32[2,4096,128]{1,2,0:T(8,128)} async-done(((f32[2,128,128]{1,2,0:T(8,128)}), f32[2,4096,128]{1,2,0:T(8,128)}) %all-gather.6.cloned.1.call-update) | async-done | bytes 4194320 | tf_op jit(solution)/shard_map/all_gather | solution.py:52
  413.1 107.1 %all-reduce.10.cloned.1.call-done = f32[2,128,128]{1,2,0:T(8,128)} async-done(((f32[2,128,128]{1,2,0:T(8,128)}), f32[2,128,128]{1,2,0:T(8,128)}) %all-reduce.10.cloned.1.call-update) | async-done | bytes 131088 | tf_op jit(solution)/shard_map/psum | solution.py:56
  521.3 83.3 %all-gather.8.cloned.1.call-done = f32[2,4096,128]{1,2,0:T(8,128)} async-done(((f32[2,128,128]{1,2,0:T(8,128)}), f32[2,4096,128]{1,2,0:T(8,128)}) %all-gather.8.cloned.1.call-update) | async-done | bytes 4194320 | tf_op jit(solution)/shard_map/all_gather | solution.py:52
  606.6 180.2 %while.11 = (s32[]{:T(128)}, f32[8,384,2,128]{3,2,1,0:T(2,128)}, s32[2,256]{1,0:T(2,128)S(1)}, s32[8]{0:T(128)S(1)}, s32[3072]{0:T(1024)}, /*index=5*/f32[2,2]{1...) while((s32[]{:T(128)}, f32[8,384,2,128]{3,2,1,0:T(2,128)}, ...), condition=%wide.region_4.5_spmd, body=%wide.region_3.4_spmd.sunk | while | flops 210962560 | bytes 3413047 | solution.py:110
  616.4 3.9 fusion.86
  624.2 3.9 fusion.84
  638.9 3.9 fusion.86
  646.7 3.9 fusion.84
  661.5 3.9 fusion.86
  669.3 3.9 fusion.84
  683.9 3.9 fusion.86
  691.7 3.9 fusion.84
  706.5 3.9 fusion.86
  714.3 3.9 fusion.84
  728.9 3.9 fusion.86
  736.7 3.9 fusion.84
  751.5 3.9 fusion.86
  759.2 3.9 fusion.84
  773.9 3.9 fusion.86
  781.7 3.9 fusion.84
  788.7 119.3 %all-reduce.12.cloned.1.call-done = f32[3072,2,128]{2,1,0:T(2,128)} async-done(((f32[3072,2,128]{2,1,0:T(2,128)}), f32[3072,2,128]{2,1,0:T(2,128)}) %all-reduce.12.cloned.1.call-update) | async-done | bytes 3145744
  (176 shorter events, 138.4 us)
Async XLA Ops:
  7.2 400.4 %copy-start = (f32[2,128,256]{2,1,0:T(8,128)S(1)}, f32[2,128,256]{2,1,0:T(8,128)}, u32[]{:S(2)}) copy-start(f32[2,128,256]{2,1,0:T(8,128)} %param.15) | copy-start | bytes 786436
  7.2 513.0 %copy-start.4 = (f32[2,256]{1,0:T(2,128)S(1)}, f32[2,256]{1,0:T(2,128)}, u32[]{:S(2)}) copy-start(f32[2,256]{1,0:T(2,128)} %param.20) | copy-start | bytes 6148
  7.2 513.1 %copy-start.5 = (f32[2,2,256]{2,1,0:T(2,128)S(1)}, f32[2,2,256]{2,1,0:T(2,128)}, u32[]{:S(2)}) copy-start(f32[2,2,256]{2,1,0:T(2,128)} %param.19) | copy-start | bytes 12292
  7.2 123.2 %all-reduce.6.cloned.1.call-start = ((), (), s32[]{:S(2)}) async-start(), calls=%async_computation | async-start | bytes 262144 | tf_op jit(solution)/shard_map/psum | solution.py:56
  12.9 593.6 %copy-start.1 = (f32[2,3072]{1,0:T(2,128)S(1)}, f32[2,3072]{1,0:T(2,128)}, u32[]{:S(2)}) copy-start(f32[2,3072]{1,0:T(2,128)} %param.22) | copy-start | bytes 73732
  12.9 593.6 %copy-start.2 = (f32[2,2]{1,0:T(2,128)S(1)}, f32[2,2]{1,0:T(2,128)}, u32[]{:S(2)}) copy-start(f32[2,2]{1,0:T(2,128)} %param.24) | copy-start | bytes 52
  12.9 593.6 %copy-start.3 = (s32[2,256]{1,0:T(2,128)S(1)}, s32[2,256]{1,0:T(2,128)}, u32[]{:S(2)}) copy-start(s32[2,256]{1,0:T(2,128)} %param.21) | copy-start | bytes 6148
  13.0 194.8 %all-gather.4.cloned.1.call-start = ((), (), s32[]{:S(2)}) async-start(), calls=%async_computation.1 | async-start | bytes 4325376 | tf_op jit(solution)/shard_map/all_gather | solution.py:52
  130.4 192.2 %all-reduce.8.cloned.1.call-start = ((), (), s32[]{:S(2)}) async-start(), calls=%async_computation.2 | async-start | bytes 262144 | tf_op jit(solution)/shard_map/psum | solution.py:56
  213.9 193.6 %all-gather.6.cloned.1.call-start = ((), (), s32[]{:S(2)}) async-start(), calls=%async_computation.3 | async-start | bytes 4325376 | tf_op jit(solution)/shard_map/all_gather | solution.py:52
  324.2 196.0 %all-reduce.10.cloned.1.call-start = ((), (), s32[]{:S(2)}) async-start(), calls=%async_computation.4 | async-start | bytes 262144 | tf_op jit(solution)/shard_map/psum | solution.py:56
  413.0 191.5 %all-gather.8.cloned.1.call-start = ((), (), s32[]{:S(2)}) async-start(), calls=%async_computation.5 | async-start | bytes 4325376 | tf_op jit(solution)/shard_map/all_gather | solution.py:52
  520.2 387.9 %all-reduce.12.cloned.1.call-start = ((), (), s32[]{:S(2)}) async-start(), calls=%async_computation.6 | async-start | bytes 6291456
Sparse Core Ops, SparseCore 0:
  13.1 117.2 all-reduce.5
  132.5 75.2 all-gather.3
  214.1 108.4 all-reduce.7
  325.0 82.4 all-gather.5
  413.1 106.9 all-reduce.9
  522.0 82.4 all-gather.7
  786.9 121.0 all-reduce.11
where the time goes:
time: 918 us; the launch traced here: 917 us
  waiting for transfers between devices  695 us (76%)
  matrix products  140 us (15%)
  other arithmetic  36.2 us (4%)
  local copies, waits for them, and re-layouts  24.9 us (3%)
  between operations  15 us (2%)
    psum x3, waiting for transfers between devices, column_total(): return lax.psum(partial_sum, 'col')  332 us
    all_gather x3, waiting for transfers between devices, to_columns(): gathered = lax.all_gather(row_block, 'row', axis=1, tiled=True)  244 us
    unnamed x8, waiting for transfers between devices  119 us
    dot_general x8, matrix products, block_term(): jnp.dot(tile_imag, src_imag, preferred_element_type=jnp.float32)  31.3 us
    dot_general x8, matrix products, block_term(): jnp.dot(tile_imag, src_real, preferred_element_type=jnp.float32)  31.3 us
    dot_general x8, matrix products, block_term(): jnp.dot(tile_real, src_imag, preferred_element_type=jnp.float32)  31 us
    dot_general x8, matrix products, block_term(): jnp.dot(tile_real, src_real, preferred_element_type=jnp.float32)  30.8 us
  transfers between devices with their start and end apart: 7, of which 7 were waited for; matrix products, arithmetic and copies ran while one was open for 0% of the time, Pallas kernels for 0%

commit v1 on v0

--- a/solution.py
+++ b/solution.py
@@ -53,7 +53,7 @@
         return lax.dynamic_slice_in_dim(gathered, lax.axis_index("col") * col_rows, col_rows, 1)
 
     def column_total(partial_sum):
-        return lax.psum(partial_sum, "col")
+        return jnp.sum(lax.all_gather(partial_sum, "col"), axis=0)
 
     top_solved = to_columns(column_total(complex_product(inv_top, rhs_top)))
     remainder = rhs_bottom - column_total(complex_product(lower_panel, top_solved))

time: 918 us -> 759 us (0.83)
  waiting for transfers between devices: 695 us -> 531 us
    psum x3 -> x0, waiting for transfers between devices: 332 us -> none  [column_total(): return lax.psum(partial_sum, 'col')]
    all_gather x0 -> x3, waiting for transfers between devices: none -> 173 us  [column_total(): return jnp.sum(lax.all_gather(partial_sum, 'col'), axis=0)]
where the time goes in v1:
time: 759 us; the launch traced here: 758 us
  waiting for transfers between devices  531 us (70%)
  matrix products  139 us (18%)
  other arithmetic  40.1 us (5%)
  local copies, waits for them, and re-layouts  26.1 us (3%)
  between operations  15.1 us (2%)
    all_gather x3, waiting for transfers between devices, to_columns(): gathered = lax.all_gather(row_block, 'row', axis=1, tiled=True)  239 us
    all_gather x3, waiting for transfers between devices, column_total(): return jnp.sum(lax.all_gather(partial_sum, 'col'), axis=0)  173 us
    unnamed x8, waiting for transfers between devices  119 us
    dot_general x8, matrix products, block_term(): jnp.dot(tile_imag, src_imag, preferred_element_type=jnp.float32)  31.3 us
    dot_general x8, matrix products, block_term(): jnp.dot(tile_imag, src_real, preferred_element_type=jnp.float32)  31.3 us
    dot_general x8, matrix products, block_term(): jnp.dot(tile_real, src_imag, preferred_element_type=jnp.float32)  31 us
    dot_general x8, matrix products, block_term(): jnp.dot(tile_real, src_real, preferred_element_type=jnp.float32)  30.8 us
    select_n x8, other arithmetic, green_tile(): lid_second = jnp.where(region == 1, lid_table[1, 1], lid_table[0, 1])  15.7 us
  transfers between devices with their start and end apart: 7, of which 7 were waited for; matrix products, arithmetic and copies ran while one was open for 0% of the time, Pallas kernels for 0%

profile of v1, /device:TPU:1, one launch (start us, length us, event | category | flops | bytes accessed | tf_op | source)
XLA Modules:
  0.0 757.9 jit_solution(17576312427497108150)
XLA Ops:
  13.1 64.0 %all-gather.16.cloned.1.call-done = f32[32,128,128]{2,1,0:T(8,128)} async-done(((f32[2,128,128]{2,1,0:T(8,128)}), f32[32,128,128]{2,1,0:T(8,128)}) %all-gather.16.cloned.1.call-update) | async-done | bytes 2097168 | tf_op jit(solution)/shard_map/all_gather | solution.py:56
  79.5 75.2 %all-gather.10.cloned.1.call-done = f32[2,4096,128]{2,1,0:T(8,128)} async-done(((f32[2,128,128]{2,1,0:T(8,128)}), f32[2,4096,128]{2,1,0:T(8,128)}) %all-gather.10.cloned.1.call-update) | async-done | bytes 4194320 | tf_op jit(solution)/shard_map/all_gather | solution.py:52
  160.9 55.1 %all-gather.18.cloned.1.call-done = f32[32,128,128]{2,1,0:T(8,128)} async-done(((f32[2,128,128]{2,1,0:T(8,128)}), f32[32,128,128]{2,1,0:T(8,128)}) %all-gather.18.cloned.1.call-update) | async-done | bytes 2097168 | tf_op jit(solution)/shard_map/all_gather | solution.py:56
  218.7 82.3 %all-gather.12.cloned.1.call-done = f32[2,4096,128]{1,2,0:T(8,128)} async-done(((f32[2,128,128]{1,2,0:T(8,128)}), f32[2,4096,128]{1,2,0:T(8,128)}) %all-gather.12.cloned.1.call-update) | async-done | bytes 4194320 | tf_op jit(solution)/shard_map/all_gather | solution.py:52
  306.5 53.8 %all-gather.20.cloned.1.call-done = f32[32,128,128]{2,1,0:T(8,128)} async-done(((f32[2,128,128]{2,1,0:T(8,128)}), f32[32,128,128]{2,1,0:T(8,128)}) %all-gather.20.cloned.1.call-update) | async-done | bytes 2097168 | tf_op jit(solution)/shard_map/all_gather | solution.py:56
  363.9 81.2 %all-gather.14.cloned.1.call-done = f32[2,4096,128]{1,2,0:T(8,128)} async-done(((f32[2,128,128]{1,2,0:T(8,128)}), f32[2,4096,128]{1,2,0:T(8,128)}) %all-gather.14.cloned.1.call-update) | async-done | bytes 4194320 | tf_op jit(solution)/shard_map/all_gather | solution.py:52
  447.1 181.1 %while.11 = (s32[]{:T(128)}, f32[8,384,2,128]{3,2,1,0:T(2,128)}, s32[2,256]{1,0:T(2,128)S(1)}, s32[8]{0:T(128)S(1)}, s32[3072]{0:T(1024)}, /*index=5*/f32[2,2]{1...) while((s32[]{:T(128)}, f32[8,384,2,128]{3,2,1,0:T(2,128)}, ...), condition=%wide.region_4.5_spmd, body=%wide.region_3.4_spmd.sunk | while | flops 210962560 | bytes 3413047 | solution.py:110
  457.1 3.9 fusion.86
  464.9 3.9 fusion.84
  479.7 3.9 fusion.86
  487.5 3.9 fusion.84
  502.3 3.9 fusion.86
  510.1 3.9 fusion.84
  524.9 3.9 fusion.86
  532.7 3.9 fusion.84
  547.5 3.9 fusion.86
  555.3 3.9 fusion.84
  570.1 3.9 fusion.86
  577.9 3.9 fusion.84
  592.7 3.9 fusion.86
  600.5 3.9 fusion.84
  615.3 3.9 fusion.86
  623.1 3.9 fusion.84
  630.1 119.3 %all-reduce.3.cloned.1.call-done = f32[3072,2,128]{2,1,0:T(2,128)} async-done(((f32[3072,2,128]{2,1,0:T(2,128)}), f32[3072,2,128]{2,1,0:T(2,128)}) %all-reduce.3.cloned.1.call-update) | async-done | bytes 3145744
  (187 shorter events, 143.3 us)
Async XLA Ops:
  7.2 147.6 %copy-start = (f32[2,128,256]{2,1,0:T(8,128)S(1)}, f32[2,128,256]{2,1,0:T(8,128)}, u32[]{:S(2)}) copy-start(f32[2,128,256]{2,1,0:T(8,128)} %param.16) | copy-start | bytes 786436
  7.2 153.7 %copy-start.3 = (f32[2,128,128]{2,1,0:T(8,128)S(1)}, f32[2,128,128]{2,1,0:T(8,128)}, u32[]{:S(2)}) copy-start(f32[2,128,128]{2,1,0:T(8,128)} %param.18) | copy-start | bytes 393220
  7.2 69.9 %all-gather.16.cloned.1.call-start = ((), (), s32[]{:S(2)}) async-start(), calls=%async_computation.3 | async-start | bytes 2228224 | tf_op jit(solution)/shard_map/all_gather | solution.py:56
  11.0 289.9 %copy-start.1 = (f32[2,128,256]{2,1,0:T(8,128)S(1)}, f32[2,128,256]{2,1,0:T(8,128)}, u32[]{:S(2)}) copy-start(f32[2,128,256]{2,1,0:T(8,128)} %param.15) | copy-start | bytes 786436
  13.0 141.8 %all-gather.10.cloned.1.call-start = ((), (), s32[]{:S(2)}) async-start(), calls=%async_computation | async-start | bytes 4325376 | tf_op jit(solution)/shard_map/all_gather | solution.py:52
  79.5 136.6 %all-gather.18.cloned.1.call-start = ((), (), s32[]{:S(2)}) async-start(), calls=%async_computation.4 | async-start | bytes 2228224 | tf_op jit(solution)/shard_map/all_gather | solution.py:56
  160.0 202.9 %copy-start.6 = (f32[2,256]{1,0:T(2,128)S(1)}, f32[2,256]{1,0:T(2,128)}, u32[]{:S(2)}) copy-start(f32[2,256]{1,0:T(2,128)} %param.20) | copy-start | bytes 6148
  160.0 202.9 %copy-start.7 = (f32[2,2,256]{2,1,0:T(2,128)S(1)}, f32[2,2,256]{2,1,0:T(2,128)}, u32[]{:S(2)}) copy-start(f32[2,2,256]{2,1,0:T(2,128)} %param.19) | copy-start | bytes 12292
  160.8 140.1 %all-gather.12.cloned.1.call-start = ((), (), s32[]{:S(2)}) async-start(), calls=%async_computation.1 | async-start | bytes 4325376 | tf_op jit(solution)/shard_map/all_gather | solution.py:52
  218.6 228.5 %copy-start.2 = (f32[2,3072]{1,0:T(2,128)S(1)}, f32[2,3072]{1,0:T(2,128)}, u32[]{:S(2)}) copy-start(f32[2,3072]{1,0:T(2,128)} %param.22) | copy-start | bytes 73732
  218.6 228.5 %copy-start.4 = (f32[2,2]{1,0:T(2,128)S(1)}, f32[2,2]{1,0:T(2,128)}, u32[]{:S(2)}) copy-start(f32[2,2]{1,0:T(2,128)} %param.24) | copy-start | bytes 52
  218.6 228.5 %copy-start.5 = (s32[2,256]{1,0:T(2,128)S(1)}, s32[2,256]{1,0:T(2,128)}, u32[]{:S(2)}) copy-start(s32[2,256]{1,0:T(2,128)} %param.21) | copy-start | bytes 6148
  218.6 141.7 %all-gather.20.cloned.1.call-start = ((), (), s32[]{:S(2)}) async-start(), calls=%async_computation.5 | async-start | bytes 2228224 | tf_op jit(solution)/shard_map/all_gather | solution.py:56
  306.5 138.6 %all-gather.14.cloned.1.call-start = ((), (), s32[]{:S(2)}) async-start(), calls=%async_computation.2 | async-start | bytes 4325376 | tf_op jit(solution)/shard_map/all_gather | solution.py:52
  362.8 386.7 %all-reduce.3.cloned.1.call-start = ((), (), s32[]{:S(2)}) async-start(), calls=%async_computation.6 | async-start | bytes 6291456
Sparse Core Ops, SparseCore 0:
  13.1 63.9 all-gather.15
  79.8 74.9 all-gather.9
  160.9 55.1 all-gather.17
  218.7 82.1 all-gather.11
  306.6 53.6 all-gather.19
  362.9 82.1 all-gather.13
  628.3 121.0 all-reduce.2
